TPU v7x, 512 devices: a whole 4x8x8 slice. The times are simulated.
512 devices in a mesh: band: 32 (over x, y), seq: 16 (over z, core).
Axes of the slice: x: 4, y: 8, z: 8, core: 2. Of those that a mesh axis runs over, the one named last changes fastest.
Arguments:
- posteriors: bfloat16 [32, 262144], P(None, ('band', 'seq'))
- seed_mask: int32 [262144], P(('band', 'seq')), may hold values 0 or 1
- frame_perm: int32 [512, 512], P(('band', 'seq')), may hold values from 0 to 511, each once within a row
- lengths: int32 [256], replicated, may hold values from 1 to 4096, 262144 in all
- embeddings: bfloat16 [262144, 256], P(('band', 'seq')), may hold values from -12 to 12
- partners: int32 [2048, 32], P(('band', 'seq')), may hold values from 0 to 127, as said below
- levels: int32 [2048, 32], P(('band', 'seq')), may hold values from 1 to 8, as said below
Outputs:
- spread_labels: float32 [32, 262144], P(None, ('band', 'seq'))
Inputs may be any that keep to these rules, and one draw needn't show every extreme that they name: `partners`: within each seq index s, slot k pairs the 128 tiles mutually: if tile number a names b in slot k then b names a in slot k; no tile names itself. `levels`: two tiles paired in slot k carry the same level.
All inputs are finite; a program needn't handle non-finite values. No bound on the sum of `seed_mask` on one device may be relied on, other than what follows from the above.
Results may differ from a plain program's by a relative error of at most 0.007.
Values may be sent and summed in bfloat16 or wider, within the bound.
No kernel may reach another device: no remote copies, remote signals or barrier semaphores. Data moves between devices by JAX's collectives and lax.ppermute only.
A program may use at most 64 MiB of HBM per device.

v0:
```python
import math
import jax
import jax.numpy as jnp
from jax import lax
from jax.sharding import PartitionSpec as P

RADIUS = 64
ITERS = 3
decay_len = 16.0
spread_rate = 0.9


def with_halo(cells, sides, width):
    for axis, dim in sides:
        count = lax.axis_size(axis)
        ends = count - 1
        head = lax.slice_in_dim(cells, 0, width, axis=dim)
        tail = lax.slice_in_dim(cells, cells.shape[dim] - width, cells.shape[dim], axis=dim)
        cells = jnp.concatenate(
            [
                lax.ppermute(tail, axis, [(i, (i + 1) % count) for i in range(ends)]),
                cells,
                lax.ppermute(head, axis, [((i + 1) % count, i) for i in range(ends)]),
            ],
            axis=dim,
        )
    return cells


def total_over_devices(values):
    for axis in ("seq", "band"):
        count = lax.axis_size(axis)
        spread = jnp.broadcast_to(values[None], (count,) + values.shape)
        rows = lax.all_to_all(spread, axis, split_axis=0, concat_axis=0, tiled=True)
        values = jnp.sum(rows, axis=0)
    return values


def band_gather(block):
    count = lax.axis_size("band")
    spread = jnp.broadcast_to(block[None], (count,) + block.shape)
    return lax.all_to_all(spread, "band", split_axis=0, concat_axis=0, tiled=True)


def on_device(posteriors, seed_mask, frame_perm, lengths, embeddings, partners, levels):
    channels, frames = posteriors.shape
    band_count = lax.axis_size("band")
    groups = lax.axis_size("seq")
    tile_count = frames // 128
    seeded = posteriors * seed_mask.astype(jnp.bfloat16)[None, :]
    ordered = jnp.take(seeded, frame_perm[0], axis=1).reshape(
        channels, band_count, frames // band_count
    )
    arrived = lax.all_to_all(ordered, "band", split_axis=1, concat_axis=1, tiled=True)
    labels = arrived.reshape(channels, frames).astype(jnp.float32)
    device = lax.axis_index("band") * groups + lax.axis_index("seq")
    frame_total = frames * band_count * groups
    window = 128 + 2 * RADIUS
    global_at = device * frames - RADIUS + jnp.arange(frames + 2 * RADIUS, dtype=jnp.int32)
    utt_ends = jnp.cumsum(lengths)
    owner_seg = jnp.sum((utt_ends[None, :] <= global_at[:, None]).astype(jnp.int32), axis=1)
    inside = (global_at >= 0) & (global_at < frame_total)
    tile_off = (jnp.arange(tile_count, dtype=jnp.int32) * 128)[:, None, None]
    win_pos = tile_off + jnp.arange(window, dtype=jnp.int32)[None, :, None]
    row_pos = tile_off + RADIUS + jnp.arange(128, dtype=jnp.int32)[None, None, :]
    offset = jnp.abs(win_pos - row_pos)
    linked = (
        (offset >= 1)
        & (offset <= RADIUS)
        & (owner_seg[win_pos] == owner_seg[row_pos])
        & inside[win_pos]
    )
    band_tiles = jnp.where(
        linked, jnp.exp(-offset.astype(jnp.float32) / decay_len), jnp.float32(0.0)
    ).astype(jnp.bfloat16)
    near_degree = jnp.sum(band_tiles.astype(jnp.float32), axis=1).reshape(frames)
    gathered = lax.all_gather(embeddings, "band", axis=0, tiled=True)
    labels_band = band_gather(arrived.reshape(channels, frames))
    labels_band, gathered = lax.optimization_barrier((labels_band, gathered))
    embed_width = embeddings.shape[1]
    partner_rows = gathered.reshape(-1, 128, embed_width)[partners]
    own_rows = embeddings.reshape(tile_count, 128, embed_width)
    inner_prod = jnp.einsum(
        "tkje,tie->tkji", partner_rows, own_rows, preferred_element_type=jnp.float32
    )
    affinity = (
        jnp.exp(0.5 * (inner_prod / math.sqrt(embed_width)))
        * (levels.astype(jnp.float32) / 8.0)[:, :, None, None]
        / 128.0
    )
    affinity = affinity.astype(jnp.bfloat16)
    far_degree = jnp.sum(affinity.astype(jnp.float32), axis=(1, 2)).reshape(frames)
    norm_scale = 1.0 / jnp.sqrt(near_degree + far_degree)

    def squares(residual):
        return total_over_devices(jnp.sum(residual * residual, axis=1))

    solution = jnp.zeros((channels, frames), jnp.float32)
    residual = labels
    direction = labels
    first_norm = jnp.sum(residual * residual, axis=1)
    scale_band = band_gather(norm_scale)
    for iteration in range(ITERS):
        lifted = (norm_scale[None, :] * direction).astype(jnp.bfloat16)
        padded = with_halo(lifted, ((("band", "seq"), 1),), RADIUS)
        windows = jnp.stack(
            [padded[:, position * 128 : position * 128 + window] for position in range(tile_count)],
            axis=0,
        )
        near_term = jnp.einsum(
            "tcw,twa->cta", windows, band_tiles, preferred_element_type=jnp.float32
        ).reshape(channels, frames)
        if iteration == 0:
            lifted_band = (scale_band[:, None, :] * labels_band.astype(jnp.float32)).astype(
                jnp.bfloat16
            )
        else:
            lifted_band = band_gather(lifted)
        spread = jnp.transpose(lifted_band, (1, 0, 2)).reshape(channels, -1, 128)
        far_tiles = spread[:, partners]
        far_term = jnp.einsum(
            "ctkj,tkji->cti", far_tiles, affinity, preferred_element_type=jnp.float32
        ).reshape(channels, frames)
        image = direction - spread_rate * norm_scale[None, :] * (near_term + far_term)
        sums = [jnp.sum(direction * image, axis=1)]
        last = iteration == ITERS - 1
        if not last:
            sums += [jnp.sum(residual * image, axis=1), jnp.sum(image * image, axis=1)]
        if iteration == 0:
            sums.append(first_norm)
        totals = total_over_devices(jnp.stack(sums))
        curve = totals[0]
        if iteration == 0:
            norm_now = totals[-1]
        alpha = norm_now / curve
        solution = solution + alpha[:, None] * direction
        if not last:
            residual = residual - alpha[:, None] * image
            norm_next = norm_now - 2.0 * alpha * totals[1] + alpha * alpha * totals[2]
            direction = residual + (norm_next / norm_now)[:, None] * direction
            norm_now = norm_next
    return solution


def solution(mesh):
    placed = (
        P(None, ("band", "seq")),
        P(("band", "seq")),
        P(("band", "seq"), None),
        P(),
        P(("band", "seq"), None),
        P(("band", "seq"), None),
        P(("band", "seq"), None),
    )
    return jax.shard_map(
        on_device, mesh=mesh, in_specs=placed, out_specs=P(None, ("band", "seq")), check_vma=False
    )
```

profile of v0, /device:TPU:1, one launch (start us, length us, event | category | flops | bytes accessed | tf_op | source)
XLA Modules:
  0.0 341.7 jit_solution(14593774616092935248)
XLA Ops:
  13.7 10.5 %all-to-all-start = ((bf16[32,2,256]{2,1,0:T(2,128)(2,1)}), bf16[32,2,256]{2,1,0:T(2,128)(2,1)S(1)}, u32[]{:S(2)}, u32[]{:S(2)}) async-start(bf16[32,2,256]{2,1,0:T(2,128)(2,1)} %reshape.829), calls=%async_computation | async-start | bytes 65536 | tf_op jit(solution)/shard_map/all_to_all | solution.py:54
  25.6 7.4 %all-to-all-done = bf16[32,2,256]{2,1,0:T(2,128)(2,1)S(1)} async-done(((bf16[32,2,256]{2,1,0:T(2,128)(2,1)}), bf16[32,2,256]{2,1,0:T(2,128)(2,1)S(1)}, u32[]{:S(2)}, u32[]{:S(2)}) %all-to-all-start) | async-done | bytes 32800 | tf_op jit(solution)/shard_map/all_to_all | solution.py:54
  34.4 3.9 %all-to-all-start.1 = ((bf16[32,32,512]{2,1,0:T(8,128)(2,1)}), bf16[32,32,512]{2,1,0:T(8,128)(2,1)S(1)}, u32[]{:S(2)}, u32[]{:S(2)}) async-start(bf16[32,32,512]{2,1,0:T(8,128)(2,1)} %broadcast_in_dim.40), calls=%async_computation.1 | async-start | bytes 2097152 | tf_op jit(solution)/shard_map/all_to_all | solution.py:42
  38.7 4.5 %gather_fusion.1 = s32[1024]{0:T(1024)S(1)} fusion(s32[640]{0:T(1024)S(1)} %convert_reduce_fusion.1, s32[1024]{0:T(1024)S(1)} %broadcast_clamp_fusion), kind=kCustom, calls=%fused_computation.1 | custom fusion | bytes 12288 | tf_op jit(solution)/shard_map/gather | solution.py:70
  45.6 6.8 %gather_fusion.3 = pred[1024]{0:T(1024)(128)(4,1)S(1)} fusion(pred[640]{0:T(1024)(128)(4,1)S(1)} %compare_and_fusion.1, s32[1024]{0:T(1024)S(1)} %broadcast_clamp_fusion), kind=kCustom, calls=%fused_computation.3 | custom fusion | bytes 6144 | tf_op jit(solution)/shard_map/gather | solution.py:71
  53.3 16.7 %all-to-all-done.1 = bf16[32,32,512]{2,1,0:T(8,128)(2,1)S(1)} async-done(((bf16[32,32,512]{2,1,0:T(8,128)(2,1)}), bf16[32,32,512]{2,1,0:T(8,128)(2,1)S(1)}, u32[]{:S(2)}, u32[]{:S(2)}) %all-to-all-start.1) | async-done | bytes 1048608 | tf_op jit(solution)/shard_map/all_to_all | solution.py:42
  70.0 58.1 %all-gather.2.cloned.1.call-done = bf16[16384,256]{1,0:T(8,128)(2,1)} async-done(((bf16[512,256]{1,0:T(8,128)(2,1)}), bf16[16384,256]{1,0:T(8,128)(2,1)}) %all-gather.2.cloned.1.call-update) | async-done | bytes 8388624 | tf_op jit(solution)/shard_map/all_gather | solution.py:77
  128.2 10.0 %gather_fusion.4 = bf16[128,128,256]{2,1,0:T(8,128)(2,1)} fusion(bf16[128,128,256]{2,1,0:T(8,128)(2,1)} %bitcast.181, s32[1024]{0:T(1024)S(1)} %pad_clamp_fusion), kind=kCustom, calls=%fused_computation.4 | custom fusion | bytes 16777728 | tf_op jit(solution)/shard_map/gather | solution.py:81
  138.1 7.7 %convert_reduce_fusion = (f32[4,128]{1,0:T(4,128)S(1)}, bf16[4,32,128,128]{3,2,1,0:T(8,128)(2,1)}) fusion(f32[4,32]{1,0:T(4,128)S(1)} %convert_multiply_fusion.6, bf16[4,32,128,256]{3,2,1,0:T(8,128)(2,1)} %bitcast.182, bf16[4,128,256,1]{2,1,3,0:T(8,128)(2,1)S(1)} %bitcast.198), kind=kOutput, calls=%fused_computation.8 | convolution fusion | flops 1086324224 | bytes 12847616 | tf_op jit(solution)/shard_map/tkje,tie->tkji/dot_general | solution.py:83
  145.9 4.2 %collective-permute-start = (bf16[32,64]{1,0:T(8,128)(2,1)S(1)}, bf16[32,64]{1,0:T(8,128)(2,1)S(1)}, u32[]{:S(2)}, u32[]{:S(2)}) collective-permute-start(bf16[32,64]{1,0:T(8,128)(2,1)S(1)} %get-tuple-element.41), channel_id=1, source_target_pairs={{0,1},{1,2},{2,3},{3,4},{4,5},{5,6},{6,7},{7,8},{8,9},{9,10},{10,1... | collective-permute-start | bytes 12296 | tf_op jit(solution)/shard_map/ppermute | solution.py:21
  152.8 5.7 %all-to-all-start.2 = ((f32[32,1,512]{2,1,0:T(1,128)}), f32[32,1,512]{2,1,0:T(1,128)S(1)}, u32[]{:S(2)}, u32[]{:S(2)}) async-start(f32[32,1,512]{2,1,0:T(1,128)} %mul.397), calls=%async_computation.2 | async-start | bytes 131072 | tf_op jit(solution)/shard_map/all_to_all | solution.py:42
  159.2 7.9 %all-to-all-done.2 = f32[32,1,512]{2,1,0:T(1,128)S(1)} async-done(((f32[32,1,512]{2,1,0:T(1,128)}), f32[32,1,512]{2,1,0:T(1,128)S(1)}, u32[]{:S(2)}, u32[]{:S(2)}) %all-to-all-start.2) | async-done | bytes 65568 | tf_op jit(solution)/shard_map/all_to_all | solution.py:42
  173.5 17.3 %all_to_all.56 = f32[16,1,128]{2,1,0:T(1,128)S(1)} all-to-all(f32[16,1,128]{2,1,0:T(1,128)S(1)} %reshape.831), channel_id=1, replica_groups=mesh['band'=32,'seq'=16] {'seq'}, dimensions={0} | all-to-all | bytes 16384 | tf_op jit(solution)/shard_map/all_to_all | solution.py:34
  192.2 11.6 %all_to_all.57 = f32[32,1,128]{2,1,0:T(1,128)S(1)} all-to-all(f32[32,1,128]{2,1,0:T(1,128)S(1)} %reshape.833), channel_id=1, replica_groups=mesh['band'=32,'seq'=16] {'band'}, dimensions={0} | all-to-all | bytes 32768 | tf_op jit(solution)/shard_map/all_to_all | solution.py:34
  205.9 3.9 %all-to-all-start.5 = ((bf16[32,32,512]{2,1,0:T(8,128)(2,1)}), bf16[32,32,512]{2,1,0:T(8,128)(2,1)S(1)}, u32[]{:S(2)}, u32[]{:S(2)}) async-start(bf16[32,32,512]{2,1,0:T(8,128)(2,1)} %broadcast_in_dim.44), calls=%async_computation.5 | async-start | bytes 2097152 | tf_op jit(solution)/shard_map/all_to_all | solution.py:42
  209.9 4.0 %collective-permute-start.2 = (bf16[32,64]{1,0:T(8,128)(2,1)S(1)}, bf16[32,64]{1,0:T(8,128)(2,1)S(1)}, u32[]{:S(2)}, u32[]{:S(2)}) collective-permute-start(bf16[32,64]{1,0:T(8,128)(2,1)S(1)} %get-tuple-element.35), channel_id=1, source_target_pairs={{0,1},{1,2},{2,3},{3,4},{4,5},{5,6},{6,7},{7,8},{8,9},{9,10},{10,1... | collective-permute-start | bytes 12296 | tf_op jit(solution)/shard_map/ppermute | solution.py:21
  219.9 14.5 %all-to-all-done.5 = bf16[32,32,512]{2,1,0:T(8,128)(2,1)S(1)} async-done(((bf16[32,32,512]{2,1,0:T(8,128)(2,1)}), bf16[32,32,512]{2,1,0:T(8,128)(2,1)S(1)}, u32[]{:S(2)}, u32[]{:S(2)}) %all-to-all-start.5) | async-done | bytes 1048608 | tf_op jit(solution)/shard_map/all_to_all | solution.py:42
  240.4 15.1 %all_to_all.58 = f32[16,3,32]{2,1,0:T(4,128)S(1)} all-to-all(f32[16,3,32]{2,1,0:T(4,128)S(1)} %broadcast_in_dim.45), channel_id=1, replica_groups=mesh['band'=32,'seq'=16] {'seq'}, dimensions={0} | all-to-all | bytes 12288 | tf_op jit(solution)/shard_map/all_to_all | solution.py:34
  255.5 14.1 %all_to_all.59 = f32[32,3,32]{2,1,0:T(4,128)S(1)} all-to-all(f32[32,3,32]{2,1,0:T(4,128)S(1)} %broadcast_in_dim.46), channel_id=1, replica_groups=mesh['band'=32,'seq'=16] {'band'}, dimensions={0} | all-to-all | bytes 24576 | tf_op jit(solution)/shard_map/all_to_all | solution.py:34
  270.9 3.9 %all-to-all-start.8 = ((bf16[32,32,512]{2,1,0:T(8,128)(2,1)}), bf16[32,32,512]{2,1,0:T(8,128)(2,1)S(1)}, u32[]{:S(2)}, u32[]{:S(2)}) async-start(bf16[32,32,512]{2,1,0:T(8,128)(2,1)} %broadcast_in_dim.47), calls=%async_computation.8 | async-start | bytes 2097152 | tf_op jit(solution)/shard_map/all_to_all | solution.py:42
  274.9 3.9 %collective-permute-start.4 = (bf16[32,64]{1,0:T(8,128)(2,1)S(1)}, bf16[32,64]{1,0:T(8,128)(2,1)S(1)}, u32[]{:S(2)}, u32[]{:S(2)}) collective-permute-start(bf16[32,64]{1,0:T(8,128)(2,1)S(1)} %get-tuple-element.29), channel_id=1, source_target_pairs={{0,1},{1,2},{2,3},{3,4},{4,5},{5,6},{6,7},{7,8},{8,9},{9,10},{10,1... | collective-permute-start | bytes 12296 | tf_op jit(solution)/shard_map/ppermute | solution.py:21
  284.7 14.7 %all-to-all-done.8 = bf16[32,32,512]{2,1,0:T(8,128)(2,1)S(1)} async-done(((bf16[32,32,512]{2,1,0:T(8,128)(2,1)}), bf16[32,32,512]{2,1,0:T(8,128)(2,1)S(1)}, u32[]{:S(2)}, u32[]{:S(2)}) %all-to-all-start.8) | async-done | bytes 1048608 | tf_op jit(solution)/shard_map/all_to_all | solution.py:42
  305.5 14.7 %all_to_all.60 = f32[16,1,32]{2,1,0:T(1,128)S(1)} all-to-all(f32[16,1,32]{2,1,0:T(1,128)S(1)} %broadcast_in_dim.48), channel_id=1, replica_groups=mesh['band'=32,'seq'=16] {'seq'}, dimensions={0} | all-to-all | bytes 4096 | tf_op jit(solution)/shard_map/all_to_all | solution.py:34
  320.2 13.9 %all_to_all.61 = f32[32,1,32]{2,1,0:T(1,128)S(1)} all-to-all(f32[32,1,32]{2,1,0:T(1,128)S(1)} %broadcast_in_dim.49), channel_id=1, replica_groups=mesh['band'=32,'seq'=16] {'band'}, dimensions={0} | all-to-all | bytes 8192 | tf_op jit(solution)/shard_map/all_to_all | solution.py:34
  (123 shorter events, 52.7 us)
Async XLA Ops:
  6.5 45.9 %copy-start.1 = (s32[4,32]{1,0:T(4,128)S(1)}, s32[4,32]{1,0:T(4,128)}, u32[]{:S(2)}) copy-start(s32[4,32]{1,0:T(4,128)} %param.12) | copy-start | bytes 1540
  6.5 46.7 %copy-start.2 = (s32[4,32]{1,0:T(4,128)S(1)}, s32[4,32]{1,0:T(4,128)}, u32[]{:S(2)}) copy-start(s32[4,32]{1,0:T(4,128)} %param.13) | copy-start | bytes 1540
  6.5 121.6 %all-gather.2.cloned.1.call-start = ((), (), s32[]{:S(2)}) async-start(), calls=%async_computation.11 | async-start | bytes 8650752 | tf_op jit(solution)/shard_map/all_gather | solution.py:77
  13.7 19.3 %all-to-all-start = ((bf16[32,2,256]{2,1,0:T(2,128)(2,1)}), bf16[32,2,256]{2,1,0:T(2,128)(2,1)S(1)}, u32[]{:S(2)}, u32[]{:S(2)}) async-start(bf16[32,2,256]{2,1,0:T(2,128)(2,1)} %reshape.829), calls=%async_computation | async-start | bytes 65536 | tf_op jit(solution)/shard_map/all_to_all | solution.py:54
  34.4 35.6 %all-to-all-start.1 = ((bf16[32,32,512]{2,1,0:T(8,128)(2,1)}), bf16[32,32,512]{2,1,0:T(8,128)(2,1)S(1)}, u32[]{:S(2)}, u32[]{:S(2)}) async-start(bf16[32,32,512]{2,1,0:T(8,128)(2,1)} %broadcast_in_dim.40), calls=%async_computation.1 | async-start | bytes 2097152 | tf_op jit(solution)/shard_map/all_to_all | solution.py:42
  128.1 10.0 %copy-start = (bf16[512,256]{1,0:T(8,128)(2,1)S(1)}, bf16[512,256]{1,0:T(8,128)(2,1)}, u32[]{:S(2)}) copy-start(bf16[512,256]{1,0:T(8,128)(2,1)} %param.11) | copy-start | bytes 786436
  145.9 12.6 %collective-permute-start = (bf16[32,64]{1,0:T(8,128)(2,1)S(1)}, bf16[32,64]{1,0:T(8,128)(2,1)S(1)}, u32[]{:S(2)}, u32[]{:S(2)}) collective-permute-start(bf16[32,64]{1,0:T(8,128)(2,1)S(1)} %get-tuple-element.41), channel_id=1, source_target_pairs={{0,1},{1,2},{2,3},{3,4},{4,5},{5,6},{6,7},{7,8},{8,9},{9,10},{10,1... | collective-permute-start | bytes 12296 | tf_op jit(solution)/shard_map/ppermute | solution.py:21
  150.2 8.4 %collective-permute-start.1 = (bf16[32,64]{1,0:T(8,128)(2,1)S(1)}, bf16[32,64]{1,0:T(8,128)(2,1)S(1)}, u32[]{:S(2)}, u32[]{:S(2)}) collective-permute-start(bf16[32,64]{1,0:T(8,128)(2,1)S(1)} %get-tuple-element.42), channel_id=1, source_target_pairs={{1,0},{2,1},{3,2},{4,3},{5,4},{6,5},{7,6},{8,7},{9,8},{10,9},{11,1... | collective-permute-start | bytes 12296 | tf_op jit(solution)/shard_map/ppermute | solution.py:23
  152.8 14.4 %all-to-all-start.2 = ((f32[32,1,512]{2,1,0:T(1,128)}), f32[32,1,512]{2,1,0:T(1,128)S(1)}, u32[]{:S(2)}, u32[]{:S(2)}) async-start(f32[32,1,512]{2,1,0:T(1,128)} %mul.397), calls=%async_computation.2 | async-start | bytes 131072 | tf_op jit(solution)/shard_map/all_to_all | solution.py:42
  205.9 28.5 %all-to-all-start.5 = ((bf16[32,32,512]{2,1,0:T(8,128)(2,1)}), bf16[32,32,512]{2,1,0:T(8,128)(2,1)S(1)}, u32[]{:S(2)}, u32[]{:S(2)}) async-start(bf16[32,32,512]{2,1,0:T(8,128)(2,1)} %broadcast_in_dim.44), calls=%async_computation.5 | async-start | bytes 2097152 | tf_op jit(solution)/shard_map/all_to_all | solution.py:42
  209.9 6.0 %collective-permute-start.2 = (bf16[32,64]{1,0:T(8,128)(2,1)S(1)}, bf16[32,64]{1,0:T(8,128)(2,1)S(1)}, u32[]{:S(2)}, u32[]{:S(2)}) collective-permute-start(bf16[32,64]{1,0:T(8,128)(2,1)S(1)} %get-tuple-element.35), channel_id=1, source_target_pairs={{0,1},{1,2},{2,3},{3,4},{4,5},{5,6},{6,7},{7,8},{8,9},{9,10},{10,1... | collective-permute-start | bytes 12296 | tf_op jit(solution)/shard_map/ppermute | solution.py:21
  213.9 5.3 %collective-permute-start.3 = (bf16[32,64]{1,0:T(8,128)(2,1)S(1)}, bf16[32,64]{1,0:T(8,128)(2,1)S(1)}, u32[]{:S(2)}, u32[]{:S(2)}) collective-permute-start(bf16[32,64]{1,0:T(8,128)(2,1)S(1)} %get-tuple-element.36), channel_id=1, source_target_pairs={{1,0},{2,1},{3,2},{4,3},{5,4},{6,5},{7,6},{8,7},{9,8},{10,9},{11,1... | collective-permute-start | bytes 12296 | tf_op jit(solution)/shard_map/ppermute | solution.py:23
  270.9 28.5 %all-to-all-start.8 = ((bf16[32,32,512]{2,1,0:T(8,128)(2,1)}), bf16[32,32,512]{2,1,0:T(8,128)(2,1)S(1)}, u32[]{:S(2)}, u32[]{:S(2)}) async-start(bf16[32,32,512]{2,1,0:T(8,128)(2,1)} %broadcast_in_dim.47), calls=%async_computation.8 | async-start | bytes 2097152 | tf_op jit(solution)/shard_map/all_to_all | solution.py:42
  274.9 6.0 %collective-permute-start.4 = (bf16[32,64]{1,0:T(8,128)(2,1)S(1)}, bf16[32,64]{1,0:T(8,128)(2,1)S(1)}, u32[]{:S(2)}, u32[]{:S(2)}) collective-permute-start(bf16[32,64]{1,0:T(8,128)(2,1)S(1)} %get-tuple-element.29), channel_id=1, source_target_pairs={{0,1},{1,2},{2,3},{3,4},{4,5},{5,6},{6,7},{7,8},{8,9},{9,10},{10,1... | collective-permute-start | bytes 12296 | tf_op jit(solution)/shard_map/ppermute | solution.py:21
  278.8 5.3 %collective-permute-start.5 = (bf16[32,64]{1,0:T(8,128)(2,1)S(1)}, bf16[32,64]{1,0:T(8,128)(2,1)S(1)}, u32[]{:S(2)}, u32[]{:S(2)}) collective-permute-start(bf16[32,64]{1,0:T(8,128)(2,1)S(1)} %get-tuple-element.30), channel_id=1, source_target_pairs={{1,0},{2,1},{3,2},{4,3},{5,4},{6,5},{7,6},{8,7},{9,8},{10,9},{11,1... | collective-permute-start | bytes 12296 | tf_op jit(solution)/shard_map/ppermute | solution.py:23
Sparse Core Ops, SparseCore 0:
  10.5 117.5 all-gather.1
where the time goes:
time: 343 us; the launch traced here: 342 us
  waiting for transfers between devices  126 us (37%)
  blocking collectives  86.7 us (25%)
  starting transfers between devices  46.1 us (13%)
  local copies, waits for them, and re-layouts  40.7 us (12%)
  matrix products  18.3 us (5%)
  between operations  13.9 us (4%)
  other arithmetic  9.58 us (3%)
    all_to_all x6, blocking collectives, total_over_devices(): rows = lax.all_to_all(spread, axis, split_axis=0, concat_axis=0, tiled=True)  86.7 us
    all_gather x1, waiting for transfers between devices, on_device(): gathered = lax.all_gather(embeddings, 'band', axis=0, tiled=True)  58.1 us
    all_to_all x4, waiting for transfers between devices, band_gather(): lax.all_to_all(spread, 'band', split_axis=0, concat_axis=0, tiled=True)  53.8 us
    all_to_all x4, starting transfers between devices, band_gather(): lax.all_to_all(spread, 'band', split_axis=0, concat_axis=0, tiled=True)  17.5 us
    ppermute x3, starting transfers between devices, with_halo(): lax.ppermute(tail, axis, [(i, (i + 1) % count) for i in range(ends)])  12.1 us
    all_to_all x1, starting transfers between devices, on_device(): lax.all_to_all(ordered, 'band', split_axis=1, concat_axis=1, tiled=True)  10.5 us
    gather x1, local copies, waits for them, and re-layouts, on_device(): partner_rows = gathered.reshape(-1, 128, embed_width)[partners]  9.99 us
    dot_general x3, matrix products, on_device(): jnp.einsum('ctkj,tkji->cti', far_tiles, affinity, preferred_element_type=...  8.82 us
  transfers between devices with their start and end apart: 12, of which 8 were waited for; matrix products, arithmetic and copies ran while one was open for 8% of the time, Pallas kernels for 0%

commit v1 on v0

--- a/solution.py
+++ b/solution.py
@@ -51,7 +51,10 @@
     ordered = jnp.take(seeded, frame_perm[0], axis=1).reshape(
         channels, band_count, frames // band_count
     )
-    arrived = lax.all_to_all(ordered, "band", split_axis=1, concat_axis=1, tiled=True)
+    arrived = jnp.concatenate(
+        lax.all_to_all(jnp.stack(jnp.split(ordered, lax.axis_size("band"), axis=1)), "band", 0, 0),
+        axis=1,
+    )
     labels = arrived.reshape(channels, frames).astype(jnp.float32)
     device = lax.axis_index("band") * groups + lax.axis_index("seq")
     frame_total = frames * band_count * groups

time: 343 us -> 343 us (level)
  blocking collectives: 86.7 us -> 106 us
  starting transfers between devices: 46.1 us -> 35.6 us
  waiting for transfers between devices: 126 us -> 118 us
    all_to_all x0 -> x1, blocking collectives: none -> 19.1 us  [on_device(): lax.all_to_all(jnp.stack(jnp.split(ordered, lax.axis_size('band'), axis=1...]
    all_to_all x1 -> x0, starting transfers between devices: 10.5 us -> none  [on_device(): lax.all_to_all(ordered, 'band', split_axis=1, concat_axis=1, tiled=True)]
    all_to_all x1 -> x0, waiting for transfers between devices: 7.39 us -> none  [on_device(): lax.all_to_all(ordered, 'band', split_axis=1, concat_axis=1, tiled=True)]
  transfers between devices with their start and end apart: 12 -> 11, of which waited for: 8 -> 7; matrix products, arithmetic and copies ran while one was open for 8% -> 8% of each run, Pallas kernels for 0% -> 0%
where the time goes in v1:
time: 343 us; the launch traced here: 342 us
  waiting for transfers between devices  118 us (34%)
  blocking collectives  106 us (31%)
  local copies, waits for them, and re-layouts  40.4 us (12%)
  starting transfers between devices  35.6 us (10%)
  matrix products  18.3 us (5%)
  between operations  14 us (4%)
  other arithmetic  10.2 us (3%)
    all_to_all x6, blocking collectives, total_over_devices(): rows = lax.all_to_all(spread, axis, split_axis=0, concat_axis=0, tiled=True)  86.7 us
    all_gather x1, waiting for transfers between devices, on_device(): gathered = lax.all_gather(embeddings, 'band', axis=0, tiled=True)  58.4 us
    all_to_all x4, waiting for transfers between devices, band_gather(): lax.all_to_all(spread, 'band', split_axis=0, concat_axis=0, tiled=True)  52 us
    all_to_all x1, blocking collectives, on_device(): lax.all_to_all(jnp.stack(jnp.split(ordered, lax.axis_size('band'), axis=1...  19.1 us
    all_to_all x4, starting transfers between devices, band_gather(): lax.all_to_all(spread, 'band', split_axis=0, concat_axis=0, tiled=True)  17.5 us
    ppermute x3, starting transfers between devices, with_halo(): lax.ppermute(tail, axis, [(i, (i + 1) % count) for i in range(ends)])  12.1 us
    gather x1, local copies, waits for them, and re-layouts, on_device(): partner_rows = gathered.reshape(-1, 128, embed_width)[partners]  9.99 us
    dot_general x3, matrix products, on_device(): jnp.einsum('ctkj,tkji->cti', far_tiles, affinity, preferred_element_type=...  8.82 us
  transfers between devices with their start and end apart: 11, of which 7 were waited for; matrix products, arithmetic and copies ran while one was open for 8% of the time, Pallas kernels for 0%

profile of v1, /device:TPU:1, one launch (start us, length us, event | category | flops | bytes accessed | tf_op | source)
XLA Modules:
  0.0 341.7 jit_solution(13605956879348965816)
XLA Ops:
  13.6 19.1 %all_to_all.56 = bf16[32,2,256]{2,1,0:T(2,128)(2,1)S(1)} all-to-all(bf16[32,2,256]{2,1,0:T(2,128)(2,1)S(1)} %reshape.908), channel_id=1, replica_groups=mesh['band'=32,'seq'=16] {'band'}, dimensions={0} | all-to-all | bytes 65536 | tf_op jit(solution)/shard_map/all_to_all | solution.py:55
  34.1 3.9 %all-to-all-start.1 = ((bf16[32,32,512]{2,1,0:T(8,128)(2,1)}), bf16[32,32,512]{2,1,0:T(8,128)(2,1)S(1)}, u32[]{:S(2)}, u32[]{:S(2)}) async-start(bf16[32,32,512]{2,1,0:T(8,128)(2,1)} %broadcast_in_dim.40), calls=%async_computation.1 | async-start | bytes 2097152 | tf_op jit(solution)/shard_map/all_to_all | solution.py:42
  40.3 4.5 %gather_fusion.1 = s32[1024]{0:T(1024)S(1)} fusion(s32[640]{0:T(1024)S(1)} %convert_reduce_fusion.1, s32[1024]{0:T(1024)S(1)} %get-tuple-element.48), kind=kCustom, calls=%fused_computation.1 | custom fusion | bytes 12288 | tf_op jit(solution)/shard_map/gather | solution.py:73
  47.3 6.8 %gather_fusion.3 = pred[1024]{0:T(1024)(128)(4,1)S(1)} fusion(pred[640]{0:T(1024)(128)(4,1)S(1)} %compare_and_fusion.1, s32[1024]{0:T(1024)S(1)} %get-tuple-element.48), kind=kCustom, calls=%fused_computation.3 | custom fusion | bytes 6144 | tf_op jit(solution)/shard_map/gather | solution.py:74
  54.8 14.9 %all-to-all-done.1 = bf16[32,32,512]{2,1,0:T(8,128)(2,1)S(1)} async-done(((bf16[32,32,512]{2,1,0:T(8,128)(2,1)}), bf16[32,32,512]{2,1,0:T(8,128)(2,1)S(1)}, u32[]{:S(2)}, u32[]{:S(2)}) %all-to-all-start.1) | async-done | bytes 1048608 | tf_op jit(solution)/shard_map/all_to_all | solution.py:42
  69.8 58.4 %all-gather.2.cloned.1.call-done = bf16[16384,256]{1,0:T(8,128)(2,1)} async-done(((bf16[512,256]{1,0:T(8,128)(2,1)}), bf16[16384,256]{1,0:T(8,128)(2,1)}) %all-gather.2.cloned.1.call-update) | async-done | bytes 8388624 | tf_op jit(solution)/shard_map/all_gather | solution.py:80
  128.1 10.0 %gather_fusion.4 = bf16[128,128,256]{2,1,0:T(8,128)(2,1)} fusion(bf16[128,128,256]{2,1,0:T(8,128)(2,1)} %bitcast.343, s32[1024]{0:T(1024)S(1)} %get-tuple-element.45), kind=kCustom, calls=%fused_computation.4 | custom fusion | bytes 16777728 | tf_op jit(solution)/shard_map/gather | solution.py:84
  138.1 7.7 %convert_reduce_fusion = (f32[4,128]{1,0:T(4,128)S(1)}, bf16[4,32,128,128]{3,2,1,0:T(8,128)(2,1)}) fusion(f32[4,32]{1,0:T(4,128)S(1)} %convert_multiply_fusion.6, bf16[4,32,128,256]{3,2,1,0:T(8,128)(2,1)} %bitcast.344, bf16[4,128,256,1]{2,1,3,0:T(8,128)(2,1)S(1)} %bitcast.360), kind=kOutput, calls=%fused_computation.8 | convolution fusion | flops 1086324224 | bytes 12847616 | tf_op jit(solution)/shard_map/tkje,tie->tkji/dot_general | solution.py:86
  145.9 4.2 %collective-permute-start = (bf16[32,64]{1,0:T(8,128)(2,1)S(1)}, bf16[32,64]{1,0:T(8,128)(2,1)S(1)}, u32[]{:S(2)}, u32[]{:S(2)}) collective-permute-start(bf16[32,64]{1,0:T(8,128)(2,1)S(1)} %get-tuple-element.41), channel_id=1, source_target_pairs={{0,1},{1,2},{2,3},{3,4},{4,5},{5,6},{6,7},{7,8},{8,9},{9,10},{10,1... | collective-permute-start | bytes 12296 | tf_op jit(solution)/shard_map/ppermute | solution.py:21
  152.8 5.7 %all-to-all-start.2 = ((f32[32,1,512]{2,1,0:T(1,128)}), f32[32,1,512]{2,1,0:T(1,128)S(1)}, u32[]{:S(2)}, u32[]{:S(2)}) async-start(f32[32,1,512]{2,1,0:T(1,128)} %mul.415), calls=%async_computation.2 | async-start | bytes 131072 | tf_op jit(solution)/shard_map/all_to_all | solution.py:42
  159.2 7.9 %all-to-all-done.2 = f32[32,1,512]{2,1,0:T(1,128)S(1)} async-done(((f32[32,1,512]{2,1,0:T(1,128)}), f32[32,1,512]{2,1,0:T(1,128)S(1)}, u32[]{:S(2)}, u32[]{:S(2)}) %all-to-all-start.2) | async-done | bytes 65568 | tf_op jit(solution)/shard_map/all_to_all | solution.py:42
  173.5 17.3 %all_to_all.57 = f32[16,1,128]{2,1,0:T(1,128)S(1)} all-to-all(f32[16,1,128]{2,1,0:T(1,128)S(1)} %reshape.910), channel_id=1, replica_groups=mesh['band'=32,'seq'=16] {'seq'}, dimensions={0} | all-to-all | bytes 16384 | tf_op jit(solution)/shard_map/all_to_all | solution.py:34
  192.2 11.6 %all_to_all.58 = f32[32,1,128]{2,1,0:T(1,128)S(1)} all-to-all(f32[32,1,128]{2,1,0:T(1,128)S(1)} %reshape.912), channel_id=1, replica_groups=mesh['band'=32,'seq'=16] {'band'}, dimensions={0} | all-to-all | bytes 32768 | tf_op jit(solution)/shard_map/all_to_all | solution.py:34
  205.9 3.9 %all-to-all-start.5 = ((bf16[32,32,512]{2,1,0:T(8,128)(2,1)}), bf16[32,32,512]{2,1,0:T(8,128)(2,1)S(1)}, u32[]{:S(2)}, u32[]{:S(2)}) async-start(bf16[32,32,512]{2,1,0:T(8,128)(2,1)} %broadcast_in_dim.44), calls=%async_computation.5 | async-start | bytes 2097152 | tf_op jit(solution)/shard_map/all_to_all | solution.py:42
  209.9 4.0 %collective-permute-start.2 = (bf16[32,64]{1,0:T(8,128)(2,1)S(1)}, bf16[32,64]{1,0:T(8,128)(2,1)S(1)}, u32[]{:S(2)}, u32[]{:S(2)}) collective-permute-start(bf16[32,64]{1,0:T(8,128)(2,1)S(1)} %get-tuple-element.35), channel_id=1, source_target_pairs={{0,1},{1,2},{2,3},{3,4},{4,5},{5,6},{6,7},{7,8},{8,9},{9,10},{10,1... | collective-permute-start | bytes 12296 | tf_op jit(solution)/shard_map/ppermute | solution.py:21
  215.8 3.3 collective-permute-done.3
  219.9 14.5 %all-to-all-done.5 = bf16[32,32,512]{2,1,0:T(8,128)(2,1)S(1)} async-done(((bf16[32,32,512]{2,1,0:T(8,128)(2,1)}), bf16[32,32,512]{2,1,0:T(8,128)(2,1)S(1)}, u32[]{:S(2)}, u32[]{:S(2)}) %all-to-all-start.5) | async-done | bytes 1048608 | tf_op jit(solution)/shard_map/all_to_all | solution.py:42
  240.5 15.1 %all_to_all.59 = f32[16,3,32]{2,1,0:T(4,128)S(1)} all-to-all(f32[16,3,32]{2,1,0:T(4,128)S(1)} %broadcast_in_dim.45), channel_id=1, replica_groups=mesh['band'=32,'seq'=16] {'seq'}, dimensions={0} | all-to-all | bytes 12288 | tf_op jit(solution)/shard_map/all_to_all | solution.py:34
  255.6 14.1 %all_to_all.60 = f32[32,3,32]{2,1,0:T(4,128)S(1)} all-to-all(f32[32,3,32]{2,1,0:T(4,128)S(1)} %broadcast_in_dim.46), channel_id=1, replica_groups=mesh['band'=32,'seq'=16] {'band'}, dimensions={0} | all-to-all | bytes 24576 | tf_op jit(solution)/shard_map/all_to_all | solution.py:34
  270.9 3.9 %all-to-all-start.8 = ((bf16[32,32,512]{2,1,0:T(8,128)(2,1)}), bf16[32,32,512]{2,1,0:T(8,128)(2,1)S(1)}, u32[]{:S(2)}, u32[]{:S(2)}) async-start(bf16[32,32,512]{2,1,0:T(8,128)(2,1)} %broadcast_in_dim.47), calls=%async_computation.8 | async-start | bytes 2097152 | tf_op jit(solution)/shard_map/all_to_all | solution.py:42
  274.9 3.9 %collective-permute-start.4 = (bf16[32,64]{1,0:T(8,128)(2,1)S(1)}, bf16[32,64]{1,0:T(8,128)(2,1)S(1)}, u32[]{:S(2)}, u32[]{:S(2)}) collective-permute-start(bf16[32,64]{1,0:T(8,128)(2,1)S(1)} %get-tuple-element.29), channel_id=1, source_target_pairs={{0,1},{1,2},{2,3},{3,4},{4,5},{5,6},{6,7},{7,8},{8,9},{9,10},{10,1... | collective-permute-start | bytes 12296 | tf_op jit(solution)/shard_map/ppermute | solution.py:21
  284.8 14.7 %all-to-all-done.8 = bf16[32,32,512]{2,1,0:T(8,128)(2,1)S(1)} async-done(((bf16[32,32,512]{2,1,0:T(8,128)(2,1)}), bf16[32,32,512]{2,1,0:T(8,128)(2,1)S(1)}, u32[]{:S(2)}, u32[]{:S(2)}) %all-to-all-start.8) | async-done | bytes 1048608 | tf_op jit(solution)/shard_map/all_to_all | solution.py:42
  305.5 14.7 %all_to_all.61 = f32[16,1,32]{2,1,0:T(1,128)S(1)} all-to-all(f32[16,1,32]{2,1,0:T(1,128)S(1)} %broadcast_in_dim.48), channel_id=1, replica_groups=mesh['band'=32,'seq'=16] {'seq'}, dimensions={0} | all-to-all | bytes 4096 | tf_op jit(solution)/shard_map/all_to_all | solution.py:34
  320.2 13.9 %all_to_all.62 = f32[32,1,32]{2,1,0:T(1,128)S(1)} all-to-all(f32[32,1,32]{2,1,0:T(1,128)S(1)} %broadcast_in_dim.49), channel_id=1, replica_groups=mesh['band'=32,'seq'=16] {'band'}, dimensions={0} | all-to-all | bytes 8192 | tf_op jit(solution)/shard_map/all_to_all | solution.py:34
  (150 shorter events, 49.7 us)
Async XLA Ops:
  6.5 48.3 %copy-start.1 = (s32[4,32]{1,0:T(4,128)S(1)}, s32[4,32]{1,0:T(4,128)}, u32[]{:S(2)}) copy-start(s32[4,32]{1,0:T(4,128)} %param.13) | copy-start | bytes 1540
  6.5 121.6 %all-gather.2.cloned.1.call-start = ((), (), s32[]{:S(2)}) async-start(), calls=%async_computation.11 | async-start | bytes 8650752 | tf_op jit(solution)/shard_map/all_gather | solution.py:80
  34.1 35.7 %all-to-all-start.1 = ((bf16[32,32,512]{2,1,0:T(8,128)(2,1)}), bf16[32,32,512]{2,1,0:T(8,128)(2,1)S(1)}, u32[]{:S(2)}, u32[]{:S(2)}) async-start(bf16[32,32,512]{2,1,0:T(8,128)(2,1)} %broadcast_in_dim.40), calls=%async_computation.1 | async-start | bytes 2097152 | tf_op jit(solution)/shard_map/all_to_all | solution.py:42
  128.1 10.0 %copy-start = (bf16[512,256]{1,0:T(8,128)(2,1)S(1)}, bf16[512,256]{1,0:T(8,128)(2,1)}, u32[]{:S(2)}) copy-start(bf16[512,256]{1,0:T(8,128)(2,1)} %param.11) | copy-start | bytes 786436
  145.9 12.6 %collective-permute-start = (bf16[32,64]{1,0:T(8,128)(2,1)S(1)}, bf16[32,64]{1,0:T(8,128)(2,1)S(1)}, u32[]{:S(2)}, u32[]{:S(2)}) collective-permute-start(bf16[32,64]{1,0:T(8,128)(2,1)S(1)} %get-tuple-element.41), channel_id=1, source_target_pairs={{0,1},{1,2},{2,3},{3,4},{4,5},{5,6},{6,7},{7,8},{8,9},{9,10},{10,1... | collective-permute-start | bytes 12296 | tf_op jit(solution)/shard_map/ppermute | solution.py:21
  150.2 8.4 %collective-permute-start.1 = (bf16[32,64]{1,0:T(8,128)(2,1)S(1)}, bf16[32,64]{1,0:T(8,128)(2,1)S(1)}, u32[]{:S(2)}, u32[]{:S(2)}) collective-permute-start(bf16[32,64]{1,0:T(8,128)(2,1)S(1)} %get-tuple-element.42), channel_id=1, source_target_pairs={{1,0},{2,1},{3,2},{4,3},{5,4},{6,5},{7,6},{8,7},{9,8},{10,9},{11,1... | collective-permute-start | bytes 12296 | tf_op jit(solution)/shard_map/ppermute | solution.py:23
  152.8 14.4 %all-to-all-start.2 = ((f32[32,1,512]{2,1,0:T(1,128)}), f32[32,1,512]{2,1,0:T(1,128)S(1)}, u32[]{:S(2)}, u32[]{:S(2)}) async-start(f32[32,1,512]{2,1,0:T(1,128)} %mul.415), calls=%async_computation.2 | async-start | bytes 131072 | tf_op jit(solution)/shard_map/all_to_all | solution.py:42
  205.9 28.5 %all-to-all-start.5 = ((bf16[32,32,512]{2,1,0:T(8,128)(2,1)}), bf16[32,32,512]{2,1,0:T(8,128)(2,1)S(1)}, u32[]{:S(2)}, u32[]{:S(2)}) async-start(bf16[32,32,512]{2,1,0:T(8,128)(2,1)} %broadcast_in_dim.44), calls=%async_computation.5 | async-start | bytes 2097152 | tf_op jit(solution)/shard_map/all_to_all | solution.py:42
  209.9 6.0 %collective-permute-start.2 = (bf16[32,64]{1,0:T(8,128)(2,1)S(1)}, bf16[32,64]{1,0:T(8,128)(2,1)S(1)}, u32[]{:S(2)}, u32[]{:S(2)}) collective-permute-start(bf16[32,64]{1,0:T(8,128)(2,1)S(1)} %get-tuple-element.35), channel_id=1, source_target_pairs={{0,1},{1,2},{2,3},{3,4},{4,5},{5,6},{6,7},{7,8},{8,9},{9,10},{10,1... | collective-permute-start | bytes 12296 | tf_op jit(solution)/shard_map/ppermute | solution.py:21
  213.9 5.3 %collective-permute-start.3 = (bf16[32,64]{1,0:T(8,128)(2,1)S(1)}, bf16[32,64]{1,0:T(8,128)(2,1)S(1)}, u32[]{:S(2)}, u32[]{:S(2)}) collective-permute-start(bf16[32,64]{1,0:T(8,128)(2,1)S(1)} %get-tuple-element.36), channel_id=1, source_target_pairs={{1,0},{2,1},{3,2},{4,3},{5,4},{6,5},{7,6},{8,7},{9,8},{10,9},{11,1... | collective-permute-start | bytes 12296 | tf_op jit(solution)/shard_map/ppermute | solution.py:23
  270.9 28.5 %all-to-all-start.8 = ((bf16[32,32,512]{2,1,0:T(8,128)(2,1)}), bf16[32,32,512]{2,1,0:T(8,128)(2,1)S(1)}, u32[]{:S(2)}, u32[]{:S(2)}) async-start(bf16[32,32,512]{2,1,0:T(8,128)(2,1)} %broadcast_in_dim.47), calls=%async_computation.8 | async-start | bytes 2097152 | tf_op jit(solution)/shard_map/all_to_all | solution.py:42
  274.9 6.0 %collective-permute-start.4 = (bf16[32,64]{1,0:T(8,128)(2,1)S(1)}, bf16[32,64]{1,0:T(8,128)(2,1)S(1)}, u32[]{:S(2)}, u32[]{:S(2)}) collective-permute-start(bf16[32,64]{1,0:T(8,128)(2,1)S(1)} %get-tuple-element.29), channel_id=1, source_target_pairs={{0,1},{1,2},{2,3},{3,4},{4,5},{5,6},{6,7},{7,8},{8,9},{9,10},{10,1... | collective-permute-start | bytes 12296 | tf_op jit(solution)/shard_map/ppermute | solution.py:21
  278.8 5.3 %collective-permute-start.5 = (bf16[32,64]{1,0:T(8,128)(2,1)S(1)}, bf16[32,64]{1,0:T(8,128)(2,1)S(1)}, u32[]{:S(2)}, u32[]{:S(2)}) collective-permute-start(bf16[32,64]{1,0:T(8,128)(2,1)S(1)} %get-tuple-element.30), channel_id=1, source_target_pairs={{1,0},{2,1},{3,2},{4,3},{5,4},{6,5},{7,6},{8,7},{9,8},{10,9},{11,1... | collective-permute-start | bytes 12296 | tf_op jit(solution)/shard_map/ppermute | solution.py:23
Sparse Core Ops, SparseCore 0:
  10.5 117.5 all-gather.1
